TPU v7x, 256 devices: a whole 4x4x8 slice. The times are simulated.
256 devices in a mesh: section: 4 (over y), fsdp: 64 (over z, x, core).
Axes of the slice: x: 4, y: 4, z: 8, core: 2. Of those that a mesh axis runs over, the one named last changes fastest.
Arguments:
- acts: bfloat16 [4, 8192, 4096], P('section', 'fsdp'), may hold values from -6 to 6
- out_grad: bfloat16 [4, 8192, 1024], P('section', 'fsdp'), may hold values from -6 to 6
- norm_gain: float32 [4, 4096], P('section'), may hold values from 0.25 to 1.75
- tiles: bfloat16 [4, 512, 4096], P('section', 'fsdp'), may hold values from -0.25 to 0.25
- tile_cols: int32 [4, 64, 8], P('section'), may hold values from 0 to 15, as said below
- tile_count: int32 [4, 64], P('section'), may hold values from 3 to 8, as said below
- tile_store_slot: int32 [4, 512], P('section'), may hold values from 0 to 511, each once within a row
Outputs:
- handed: bfloat16 [4, 8192, 4096], P('section', 'fsdp')
- weight_grad: float32 [4, 512, 4096], P('section', 'fsdp')
Inputs may be any that keep to these rules, and one draw needn't show every extreme that they name: `tile_cols`: within a row panel the listed block columns are all different. `tile_count`: every section has a panel with exactly 8 and a panel with exactly 3 kept tiles. `tile_store_slot`: each section's row is a permutation of the slots.
All inputs are finite; a program needn't handle non-finite values.
Results may differ from a plain program's by a relative error of at most 0.0029.
Values may be sent and summed in bfloat16 or wider, within the bound.
No kernel may reach another device: no remote copies, remote signals or barrier semaphores. Data moves between devices by JAX's collectives and lax.ppermute only.
A program may use at most 128 MiB of HBM per device.

v0:
```python
import jax
import jax.numpy as jnp
from jax import lax
from jax.sharding import PartitionSpec as P

EPS = 1e-05


def shifted(value, axis, steps):
    count = lax.axis_size(axis)
    leading, last = (max(0, -steps), min(count, count - steps))
    return lax.ppermute(value, axis, [(source, source + steps) for source in range(leading, last)])


def local(acts, out_grad, norm_gain, tiles, tile_cols, tile_count, tile_store_slot):
    inputs_f = acts[0].astype(jnp.float32)
    key_grad = out_grad[0]
    gain_row = norm_gain[0]
    column_list = tile_cols[0]
    count_list = tile_count[0]
    slot_lookup = tile_store_slot[0]
    tok_rows, width = inputs_f.shape
    kv_width = key_grad.shape[1]
    panel_list, most_kept = column_list.shape
    blk = width // panel_list
    ncol = kv_width // blk
    store_slots = panel_list * most_kept
    area = blk * blk
    slot_dev = tiles.shape[1]
    grad_scale = (tok_rows * lax.axis_size("zx") * lax.axis_size("core")) ** (-0.5)
    tile_positions = jnp.arange(store_slots, dtype=jnp.int32)
    inverse_order = jnp.zeros((store_slots,), jnp.int32).at[slot_lookup].set(tile_positions)
    kept_grid = jnp.arange(most_kept)[None, :] < count_list[:, None]
    mean_sq = jnp.mean(inputs_f * inputs_f, axis=1, keepdims=True)
    recip = lax.rsqrt(mean_sq + EPS)
    normed = (inputs_f * recip * gain_row[None, :]).astype(jnp.bfloat16)
    zx_size = lax.axis_size("zx")
    core_size = lax.axis_size("core")
    gathered = lax.all_gather(tiles[0], "zx", axis=0, tiled=True)
    gathered = lax.all_gather(gathered, "core", axis=0, tiled=True)
    slot_ids = jnp.arange(store_slots, dtype=jnp.int32)
    slot_dev_i = slot_ids // (slot_dev * core_size)
    slot_core = slot_ids // slot_dev % core_size
    row_of_slot = slot_core * (zx_size * slot_dev) + slot_dev_i * slot_dev + slot_ids % slot_dev
    placed = gathered[row_of_slot[slot_lookup]].reshape(panel_list, most_kept, blk, blk)
    grad_padded = jnp.concatenate(
        [key_grad.reshape(tok_rows, ncol, blk), jnp.zeros((tok_rows, 1, blk), key_grad.dtype)],
        axis=1,
    )
    safe_cols = jnp.where(kept_grid, column_list, ncol)
    selected = grad_padded[:, safe_cols]
    normed_grad = jnp.einsum(
        "tpkb,pkab->tpa", selected, placed, preferred_element_type=jnp.float32
    ).reshape(tok_rows, width)
    normed_blocks = normed.reshape(tok_rows, panel_list, blk)
    terms_pos = jnp.einsum(
        "tpa,tpkb->pkab", normed_blocks, selected, preferred_element_type=jnp.float32
    )
    terms_pos = (terms_pos * grad_scale).reshape(store_slots, area)
    scaled = gain_row[None, :] * normed_grad
    inner = jnp.sum(scaled * inputs_f, axis=1, keepdims=True) / width
    input_grad = (recip * scaled - inputs_f * recip**3 * inner).astype(jnp.bfloat16)
    order_k = jnp.arange(core_size)[:, None, None]
    order_i = jnp.arange(zx_size)[None, :, None]
    order_j = jnp.arange(slot_dev)[None, None, :]
    rs_order = ((order_i * core_size + order_k) * slot_dev + order_j).reshape(-1)
    weight_grad = lax.psum_scatter(
        terms_pos[inverse_order[rs_order]], "core", scatter_dimension=0, tiled=True
    )
    weight_grad = lax.psum_scatter(weight_grad, "zx", scatter_dimension=0, tiled=True)
    handed = shifted(input_grad, "section", -1)
    return (handed[None], weight_grad[None])


def solution(mesh):
    sec, fs = mesh.devices.shape
    mesh = jax.sharding.Mesh(mesh.devices.reshape(sec, fs // 2, 2), ("section", "zx", "core"))
    F = ("zx", "core")
    placed = (
        P("section", F, None),
        P("section", F, None),
        P("section", None),
        P("section", F, None),
        P("section", None, None),
        P("section", None),
        P("section", None),
    )
    return jax.shard_map(
        local,
        mesh=mesh,
        in_specs=placed,
        out_specs=(P("section", F, None), P("section", F, None)),
        check_vma=False,
    )
```

profile of v0, /device:TPU:8, one launch (start us, length us, event | category | flops | bytes accessed | tf_op | source)
XLA Modules:
  0.0 460.3 jit_solution(11396080284697945354)
XLA Ops:
  7.2 0.0 copy-start.2
  7.2 0.0 copy-start.3
  7.2 0.0 all-gather.5.cloned.1.call-start
  7.2 0.7 all-gather.5.cloned.1.call-update
  7.9 0.0 all-gather.7.cloned.1.call-start
  8.0 83.4 %all-gather.5.cloned.1.call-done = bf16[1,256,4096]{2,1,0:T(8,128)(2,1)} async-done(((bf16[1,8,4096]{2,1,0:T(8,128)(2,1)}), bf16[1,256,4096]{2,1,0:T(8,128)(2,1)}) %all-gather.5.cloned.1.call-update) | async-done | bytes 2097168 | tf_op jit(solution)/shard_map/all_gather | solution.py:39
  91.4 0.0 all-gather.7.cloned.1.call-update
  91.4 0.0 reduce-scatter.3.cloned.1.call-start
  91.5 1.1 copy.12
  92.6 0.7 compare_select_fusion.4
  93.3 0.1 copy.13
  93.4 0.1 reshape.243
  93.5 1.5 copy.15
  95.0 0.5 broadcast.221
  95.5 0.0 copy-done.2
  95.5 0.7 reduce.4
  96.2 0.1 mul.116
  96.2 0.1 iota_add_fusion
  96.3 0.1 add.150
  96.4 0.0 copy-done.3
  96.5 3.5 gather_fusion
  100.0 0.0 copy-start.1
  100.0 13.4 %gather_fusion.2 = bf16[512,128,64]{1,2,0:T(8,128)(2,1)} fusion(bf16[128,17,64]{0,2,1:T(8,128)(2,1)S(1)} %concatenate.3, s32[1024]{0:T(1024)S(1)} %pad_clamp_fusion.2), kind=kCustom, calls=%fused_computation.2 | custom fusion | bytes 16779264 | tf_op jit(solution)/shard_map/gather | solution.py:51
  113.4 2.6 scatter_custom_fusion
  116.0 3.5 gather_fusion.3
  119.6 0.0 copy-done.1
  119.6 0.3 fusion.2
  119.9 0.0 all-gather.7.cloned.1.call-done
  119.9 11.3 %gather_fusion.1 = bf16[512,4096]{1,0:T(8,128)(2,1)} fusion(bf16[512,4096]{1,0:T(8,128)(2,1)} %bitcast.58, s32[1024]{0:T(1024)S(1)} %pad_clamp_fusion.3), kind=kCustom, calls=%fused_computation.1 | custom fusion | bytes 8390656 | tf_op jit(solution)/shard_map/gather | solution.py:45
  131.2 12.6 %reshape.220 = bf16[64,8,64,64]{3,2,1,0:T(8,128)(2,1)} reshape(bf16[512,4096]{1,0:T(8,128)(2,1)} %gather_fusion.1) | data formatting | bytes 8388608 | tf_op jit(solution)/shard_map/reshape | solution.py:45
  143.8 9.3 %fusion.1 = (f32[128]{0:T(128)S(1)}, f32[64,64,128,1]{2,1,3,0:T(8,128)}) fusion(f32[128,64,64]{0,2,1:T(8,128)S(1)} %bitcast.63, f32[64,64]{1,0:T(8,128)S(1)} %mul.116, bf16[64,8,64,64]{3,2,1,0:T(8,128)(2,1)} %reshape.220, bf16[128,64,8,64]{0,3,2,1:T(8,128)(2,1)} %bitcast.59), kind=kOutput, calls=%fused_computation.9 | convolution fusion | flops 538443648 | bytes 16794112 | tf_op jit(solution)/shard_map/tpkb,pkab->tpa/dot_general | solution.py:52
  153.1 0.0 slice-done
  153.1 0.0 slice-done.1
  153.1 7.1 %multiply_bitcast_fusion = f32[64,8,64,64]{2,3,1,0:T(8,128)} fusion(bf16[128,64,8,64]{0,3,2,1:T(8,128)(2,1)S(1)} %bitcast.62, f32[128,64,64]{0,2,1:T(8,128)S(1)} %bitcast.64, f32[128]{0:T(128)S(1)} %get-tuple-element.2, f32[64,64]{1,0:T(8,128)S(1)} %mul.116), kind=kOutput, calls=%fused_computation.6 | convolution fusion | flops 540540928 | bytes 18891264 | tf_op jit(solution)/shard_map/tpa,tpkb->pkab/dot_general | solution.py:56
  160.2 17.4 %copy.16 = f32[64,8,64,64]{3,2,1,0:T(8,128)} copy(f32[64,8,64,64]{2,3,1,0:T(8,128)} %multiply_bitcast_fusion) | data formatting | bytes 16777216 | tf_op jit(solution)/shard_map/mul | solution.py:59
  177.6 14.8 %reshape.222 = f32[512,4096]{1,0:T(8,128)} reshape(f32[64,8,64,64]{3,2,1,0:T(8,128)} %copy.16) | data formatting | bytes 16777216 | tf_op jit(solution)/shard_map/reshape | solution.py:59
  192.4 12.2 %gather_fusion.4 = f32[512,4096]{1,0:T(8,128)} fusion(f32[512,4096]{1,0:T(8,128)} %reshape.222, s32[1024]{0:T(1024)S(1)} %pad_clamp_fusion), kind=kCustom, calls=%fused_computation.4 | custom fusion | bytes 16779264 | tf_op jit(solution)/shard_map/gather | solution.py:68
  204.6 0.0 reduce-scatter.3.cloned.1.call-update
  204.7 0.0 copy-start
  204.7 0.0 reduce-scatter.5.cloned.1.call-start
  204.7 19.2 %reduce-scatter.3.cloned.1.call-done = f32[256,4096]{1,0:T(8,128)} async-done(((f32[512,4096]{1,0:T(8,128)}), f32[256,4096]{1,0:T(8,128)}) %reduce-scatter.3.cloned.1.call-update) | async-done | bytes 4194320 | tf_op jit(solution)/shard_map/reduce_scatter | solution.py:67
  223.9 0.0 reduce-scatter.5.cloned.1.call-update
  223.9 1.9 copy.14
  225.8 2.2 fusion.5
  228.0 2.7 collective-permute-start
  230.7 24.4 %collective-permute-done = bf16[128,4096]{1,0:T(8,128)(2,1)S(1)} collective-permute-done((bf16[128,4096]{1,0:T(8,128)(2,1)S(1)}, bf16[128,4096]{1,0:T(8,128)(2,1)S(1)}, u32[]{:S(2)}, u32[]{:S(2)}) %collective-permute-start) | collective-permute-done | bytes 1048608 | tf_op jit(solution)/shard_map/ppermute | solution.py:12
  255.1 197.6 %reduce-scatter.5.cloned.1.call-done = f32[8,4096]{1,0:T(8,128)} async-done(((f32[256,4096]{1,0:T(8,128)}), f32[8,4096]{1,0:T(8,128)}) %reduce-scatter.5.cloned.1.call-update) | async-done | bytes 131088 | tf_op jit(solution)/shard_map/reduce_scatter | solution.py:70
  452.8 1.0 copy.20
  (19 shorter events, 0.1 us)
Async XLA Ops:
  7.2 88.3 %copy-start.2 = (f32[1,4096]{1,0:T(1,128)S(1)}, f32[1,4096]{1,0:T(1,128)}, u32[]{:S(2)}) copy-start(f32[1,4096]{1,0:T(1,128)} %param.9) | copy-start | bytes 49156
  7.2 89.3 %copy-start.3 = (s32[1,512]{1,0:T(1,128)S(1)}, s32[1,512]{1,0:T(1,128)}, u32[]{:S(2)}) copy-start(s32[1,512]{1,0:T(1,128)} %param.13) | copy-start | bytes 6148
  7.2 84.2 %all-gather.5.cloned.1.call-start = ((), (), s32[]{:S(2)}) async-start(), calls=%async_computation.4 | async-start | bytes 2162688 | tf_op jit(solution)/shard_map/all_gather | solution.py:39
  7.9 112.0 %all-gather.7.cloned.1.call-start = ((), (), s32[]{:S(2)}) async-start(), calls=%async_computation.5 | async-start | bytes 6291456 | tf_op jit(solution)/shard_map/all_gather | solution.py:40
  91.4 132.5 %reduce-scatter.3.cloned.1.call-start = ((), (), s32[]{:S(2)}) async-start(), calls=%async_computation.2 | async-start | bytes 12582912 | tf_op jit(solution)/shard_map/reduce_scatter | solution.py:67
  100.0 19.6 %copy-start.1 = (bf16[1,128,4096]{2,1,0:T(8,128)(2,1)S(1)}, bf16[1,128,4096]{2,1,0:T(8,128)(2,1)}, u32[]{:S(2)}) copy-start(bf16[1,128,4096]{2,1,0:T(8,128)(2,1)} %param.7) | copy-start | bytes 3145732
  143.8 9.3 %slice-start = ((s8[8388608]{0:T(1024)(128)(4,1)}), s8[4194304]{0:T(1024)(128)(4,1)S(1)}, s32[]{:S(2)}) async-start(s8[8388608]{0:T(1024)(128)(4,1)} %bitcast.60), calls=%async_computation.6 | async-start | bytes 8388608
  143.8 9.3 %slice-start.1 = ((s8[8388608]{0:T(1024)(128)(4,1)}), s8[4194304]{0:T(1024)(128)(4,1)S(1)}, s32[]{:S(2)}) async-start(s8[8388608]{0:T(1024)(128)(4,1)} %bitcast.60), calls=%async_computation.7 | async-start | bytes 8388608
  204.7 19.2 %copy-start = (f32[64,64,128,1]{2,1,3,0:T(8,128)S(1)}, f32[64,64,128,1]{2,1,3,0:T(8,128)}, u32[]{:S(2)}) copy-start(f32[64,64,128,1]{2,1,3,0:T(8,128)} %get-tuple-element.5) | copy-start | bytes 6291460
  204.7 248.1 %reduce-scatter.5.cloned.1.call-start = ((), (), s32[]{:S(2)}) async-start(), calls=%async_computation.3 | async-start | bytes 4325376 | tf_op jit(solution)/shard_map/reduce_scatter | solution.py:70
  228.0 27.1 %collective-permute-start = (bf16[128,4096]{1,0:T(8,128)(2,1)S(1)}, bf16[128,4096]{1,0:T(8,128)(2,1)S(1)}, u32[]{:S(2)}, u32[]{:S(2)}) collective-permute-start(bf16[128,4096]{1,0:T(8,128)(2,1)S(1)} %fusion.5), channel_id=1, source_target_pairs={{64,0},{128,64},{192,128},{65,1},{129,65},{193,129},{66,2},{130,66... | collective-permute-start | bytes 3145736 | tf_op jit(solution)/shard_map/ppermute | solution.py:12
Sparse Core Ops, SparseCore 0:
  10.6 80.7 all-gather.4
  93.2 16.2 all-gather.6
  204.8 19.0 reduce-scatter.2
  228.2 224.5 reduce-scatter.4
where the time goes:
time: 461 us; the launch traced here: 460 us
  waiting for transfers between devices  325 us (70%)
  local copies, waits for them, and re-layouts  97.6 us (21%)
  matrix products  16.4 us (4%)
  between operations  14 us (3%)
    reduce_scatter x1, waiting for transfers between devices, local(): lax.psum_scatter(weight_grad, 'zx', scatter_dimension=0, tiled=True)  198 us
    all_gather x1, waiting for transfers between devices, local(): gathered = lax.all_gather(tiles[0], 'zx', axis=0, tiled=True)  83.4 us
    ppermute x1, waiting for transfers between devices, shifted(): lax.ppermute(value, axis, [(source, source + steps) for source in range(l...  24.4 us
    reduce_scatter x1, waiting for transfers between devices, local(): lax.psum_scatter(terms_pos[inverse_order[rs_order]], 'core', scatter_dime...  19.2 us
    mul x1, local copies, waits for them, and re-layouts, local(): terms_pos = (terms_pos * grad_scale).reshape(store_slots, area)  17.4 us
    reshape x1, local copies, waits for them, and re-layouts, local(): terms_pos = (terms_pos * grad_scale).reshape(store_slots, area)  14.8 us
    gather x1, local copies, waits for them, and re-layouts, local(): selected = grad_padded[:, safe_cols]  13.4 us
    reshape x1, local copies, waits for them, and re-layouts, local(): gathered[row_of_slot[slot_lookup]].reshape(panel_list, most_kept, blk, blk)  12.6 us
  transfers between devices with their start and end apart: 5, of which 4 were waited for; matrix products, arithmetic and copies ran while one was open for 7% of the time, Pallas kernels for 0%

commit v1 on v0

--- a/solution.py
+++ b/solution.py
@@ -36,7 +36,9 @@
     normed = (inputs_f * recip * gain_row[None, :]).astype(jnp.bfloat16)
     zx_size = lax.axis_size("zx")
     core_size = lax.axis_size("core")
-    gathered = lax.all_gather(tiles[0], "zx", axis=0, tiled=True)
+    gathered = jnp.concatenate(
+        lax.all_to_all(jnp.stack([tiles[0]] * lax.axis_size("zx")), "zx", 0, 0), axis=0
+    )
     gathered = lax.all_gather(gathered, "core", axis=0, tiled=True)
     slot_ids = jnp.arange(store_slots, dtype=jnp.int32)
     slot_dev_i = slot_ids // (slot_dev * core_size)

time: 461 us -> 439 us (0.952)
  waiting for transfers between devices: 325 us -> 242 us
  blocking collectives: 0 us -> 61.7 us
    all_gather x1 -> x0, waiting for transfers between devices: 83.4 us -> none  [local(): gathered = lax.all_gather(tiles[0], 'zx', axis=0, tiled=True)]
    all_to_all x0 -> x1, blocking collectives: none -> 61.7 us  [local(): lax.all_to_all(jnp.stack([tiles[0]] * lax.axis_size('zx')), 'zx', 0, 0)]
  transfers between devices with their start and end apart: 5 -> 4, of which waited for: 4 -> 3; matrix products, arithmetic and copies ran while one was open for 7% -> 7% of each run, Pallas kernels for 0% -> 0%
where the time goes in v1:
time: 439 us; the launch traced here: 438 us
  waiting for transfers between devices  242 us (55%)
  local copies, waits for them, and re-layouts  98.5 us (22%)
  blocking collectives  61.7 us (14%)
  matrix products  16.4 us (4%)
  between operations  14 us (3%)
    reduce_scatter x1, waiting for transfers between devices, local(): lax.psum_scatter(weight_grad, 'zx', scatter_dimension=0, tiled=True)  198 us
    all_to_all x1, blocking collectives, local(): lax.all_to_all(jnp.stack([tiles[0]] * lax.axis_size('zx')), 'zx', 0, 0)  61.7 us
    ppermute x1, waiting for transfers between devices, shifted(): lax.ppermute(value, axis, [(source, source + steps) for source in range(l...  24.4 us
    reduce_scatter x1, waiting for transfers between devices, local(): lax.psum_scatter(terms_pos[inverse_order[rs_order]], 'core', scatter_dime...  19.1 us
    mul x1, local copies, waits for them, and re-layouts, local(): terms_pos = (terms_pos * grad_scale).reshape(store_slots, area)  17.4 us
    reshape x1, local copies, waits for them, and re-layouts, local(): terms_pos = (terms_pos * grad_scale).reshape(store_slots, area)  14.8 us
    gather x1, local copies, waits for them, and re-layouts, local(): selected = grad_padded[:, safe_cols]  13.4 us
    reshape x1, local copies, waits for them, and re-layouts, local(): gathered[row_of_slot[slot_lookup]].reshape(panel_list, most_kept, blk, blk)  12.6 us
  transfers between devices with their start and end apart: 4, of which 3 were waited for; matrix products, arithmetic and copies ran while one was open for 7% of the time, Pallas kernels for 0%

profile of v1, /device:TPU:8, one launch (start us, length us, event | category | flops | bytes accessed | tf_op | source)
XLA Modules:
  0.0 438.4 jit_solution(12646975113457193823)
XLA Ops:
  7.2 0.0 all-gather.2.cloned.1.call-start
  7.2 0.0 copy-start.2
  7.2 0.0 copy-start.4
  7.2 0.0 copy-start.6
  7.2 0.0 copy-start.1
  7.3 1.2 stack.3
  8.4 0.0 copy-start.3
  8.4 0.0 copy-start.5
  8.4 61.7 %all_to_all.5 = bf16[32,8,4096]{2,1,0:T(8,128)(2,1)} all-to-all(bf16[32,8,4096]{2,1,0:T(8,128)(2,1)S(1)} %stack.3), channel_id=1, replica_groups=mesh['section'=4,'zx'=32,'core'=2] {'zx'}, dimensions={0} | all-to-all | bytes 4194304 | tf_op jit(solution)/shard_map/all_to_all | solution.py:40
  70.2 0.0 all-gather.2.cloned.1.call-update
  70.2 0.0 reduce-scatter.3.cloned.1.call-start
  70.3 0.0 copy-done.2
  70.3 0.8 copy.12
  71.1 0.0 copy-done.4
  71.1 0.0 copy-done.6
  71.1 0.1 copy.13
  71.2 0.1 reshape.248
  71.3 0.5 copy.15
  71.8 0.5 broadcast.222
  72.4 0.7 reduce.4
  73.1 0.1 mul.116
  73.1 0.1 iota_add_fusion
  73.2 0.1 add.150
  73.4 3.5 gather_fusion
  76.9 1.0 concatenate.3
  77.9 13.4 %gather_fusion.2 = bf16[512,128,64]{1,2,0:T(8,128)(2,1)} fusion(bf16[128,17,64]{0,2,1:T(8,128)(2,1)S(1)} %concatenate.3, s32[1024]{0:T(1024)S(1)} %pad_clamp_fusion.2), kind=kCustom, calls=%fused_computation.2 | custom fusion | bytes 16779264 | tf_op jit(solution)/shard_map/gather | solution.py:53
  91.2 2.6 scatter_custom_fusion
  93.9 3.5 gather_fusion.3
  97.4 0.3 fusion.2
  97.7 0.0 all-gather.2.cloned.1.call-done
  97.7 11.3 %gather_fusion.1 = bf16[512,4096]{1,0:T(8,128)(2,1)} fusion(bf16[512,4096]{1,0:T(8,128)(2,1)} %all-gather.2.cloned.1.call-done, s32[1024]{0:T(1024)S(1)} %pad_clamp_fusion.3), kind=kCustom, calls=%fused_computation.1 | custom fusion | bytes 8390656 | tf_op jit(solution)/shard_map/gather | solution.py:47
  109.0 12.6 %reshape.225 = bf16[64,8,64,64]{3,2,1,0:T(8,128)(2,1)} reshape(bf16[512,4096]{1,0:T(8,128)(2,1)} %gather_fusion.1) | data formatting | bytes 8388608 | tf_op jit(solution)/shard_map/reshape | solution.py:47
  121.6 9.3 %fusion.1 = (f32[128]{0:T(128)S(1)}, f32[64,64,128,1]{2,1,3,0:T(8,128)}) fusion(f32[128,64,64]{0,2,1:T(8,128)S(1)} %bitcast.63, f32[64,64]{1,0:T(8,128)S(1)} %mul.116, bf16[64,8,64,64]{3,2,1,0:T(8,128)(2,1)} %reshape.225, bf16[128,64,8,64]{0,3,2,1:T(8,128)(2,1)} %bitcast.59), kind=kOutput, calls=%fused_computation.9 | convolution fusion | flops 538443648 | bytes 16794112 | tf_op jit(solution)/shard_map/tpkb,pkab->tpa/dot_general | solution.py:54
  131.0 7.1 %multiply_bitcast_fusion = f32[64,8,64,64]{2,3,1,0:T(8,128)} fusion(bf16[128,64,8,64]{0,3,2,1:T(8,128)(2,1)S(1)} %bitcast.62, f32[128,64,64]{0,2,1:T(8,128)S(1)} %bitcast.64, f32[128]{0:T(128)S(1)} %get-tuple-element.2, f32[64,64]{1,0:T(8,128)S(1)} %mul.116), kind=kOutput, calls=%fused_computation.6 | convolution fusion | flops 540540928 | bytes 18891264 | tf_op jit(solution)/shard_map/tpa,tpkb->pkab/dot_general | solution.py:58
  138.0 17.4 %copy.16 = f32[64,8,64,64]{3,2,1,0:T(8,128)} copy(f32[64,8,64,64]{2,3,1,0:T(8,128)} %multiply_bitcast_fusion) | data formatting | bytes 16777216 | tf_op jit(solution)/shard_map/mul | solution.py:61
  155.5 14.8 %reshape.227 = f32[512,4096]{1,0:T(8,128)} reshape(f32[64,8,64,64]{3,2,1,0:T(8,128)} %copy.16) | data formatting | bytes 16777216 | tf_op jit(solution)/shard_map/reshape | solution.py:61
  170.2 12.2 %gather_fusion.4 = f32[512,4096]{1,0:T(8,128)} fusion(f32[512,4096]{1,0:T(8,128)} %reshape.227, s32[1024]{0:T(1024)S(1)} %pad_clamp_fusion), kind=kCustom, calls=%fused_computation.4 | custom fusion | bytes 16779264 | tf_op jit(solution)/shard_map/gather | solution.py:70
  182.5 0.0 reduce-scatter.3.cloned.1.call-update
  182.5 0.0 copy-start
  182.5 0.0 reduce-scatter.5.cloned.1.call-start
  182.5 19.1 %reduce-scatter.3.cloned.1.call-done = f32[256,4096]{1,0:T(8,128)} async-done(((f32[512,4096]{1,0:T(8,128)}), f32[256,4096]{1,0:T(8,128)}) %reduce-scatter.3.cloned.1.call-update) | async-done | bytes 4194320 | tf_op jit(solution)/shard_map/reduce_scatter | solution.py:69
  201.6 0.0 reduce-scatter.5.cloned.1.call-update
  201.6 1.9 copy.14
  203.5 2.2 fusion.5
  205.7 2.7 collective-permute-start
  208.4 24.4 %collective-permute-done = bf16[128,4096]{1,0:T(8,128)(2,1)S(1)} collective-permute-done((bf16[128,4096]{1,0:T(8,128)(2,1)S(1)}, bf16[128,4096]{1,0:T(8,128)(2,1)S(1)}, u32[]{:S(2)}, u32[]{:S(2)}) %collective-permute-start) | collective-permute-done | bytes 1048608 | tf_op jit(solution)/shard_map/ppermute | solution.py:12
  232.9 198.0 %reduce-scatter.5.cloned.1.call-done = f32[8,4096]{1,0:T(8,128)} async-done(((f32[256,4096]{1,0:T(8,128)}), f32[8,4096]{1,0:T(8,128)}) %reduce-scatter.5.cloned.1.call-update) | async-done | bytes 131088 | tf_op jit(solution)/shard_map/reduce_scatter | solution.py:72
  430.9 1.0 copy.20
  (24 shorter events, 0.1 us)
Async XLA Ops:
  7.2 90.6 %all-gather.2.cloned.1.call-start = ((), (), s32[]{:S(2)}) async-start(), calls=%async_computation.3 | async-start | bytes 6291456 | tf_op jit(solution)/shard_map/all_gather | solution.py:42
  7.2 63.1 %copy-start.2 = (bf16[1,128,1024]{2,1,0:T(8,128)(2,1)S(1)}, bf16[1,128,1024]{2,1,0:T(8,128)(2,1)}, u32[]{:S(2)}) copy-start(bf16[1,128,1024]{2,1,0:T(8,128)(2,1)} %param.8) | copy-start | bytes 786436
  7.2 63.9 %copy-start.4 = (s32[1,64,8]{1,2,0:T(8,128)S(1)}, s32[1,64,8]{1,2,0:T(8,128)}, u32[]{:S(2)}) copy-start(s32[1,64,8]{1,2,0:T(8,128)} %param.11) | copy-start | bytes 6148
  7.2 63.9 %copy-start.6 = (s32[1,64]{1,0:T(1,128)S(1)}, s32[1,64]{1,0:T(1,128)}, u32[]{:S(2)}) copy-start(s32[1,64]{1,0:T(1,128)} %param.12) | copy-start | bytes 772
  7.2 64.1 %copy-start.1 = (bf16[1,128,4096]{2,1,0:T(8,128)(2,1)S(1)}, bf16[1,128,4096]{2,1,0:T(8,128)(2,1)}, u32[]{:S(2)}) copy-start(bf16[1,128,4096]{2,1,0:T(8,128)(2,1)} %param.7) | copy-start | bytes 3145732
  8.4 63.9 %copy-start.3 = (f32[1,4096]{1,0:T(1,128)S(1)}, f32[1,4096]{1,0:T(1,128)}, u32[]{:S(2)}) copy-start(f32[1,4096]{1,0:T(1,128)} %param.9) | copy-start | bytes 49156
  8.4 64.9 %copy-start.5 = (s32[1,512]{1,0:T(1,128)S(1)}, s32[1,512]{1,0:T(1,128)}, u32[]{:S(2)}) copy-start(s32[1,512]{1,0:T(1,128)} %param.13) | copy-start | bytes 6148
  70.2 131.4 %reduce-scatter.3.cloned.1.call-start = ((), (), s32[]{:S(2)}) async-start(), calls=%async_computation.4 | async-start | bytes 12582912 | tf_op jit(solution)/shard_map/reduce_scatter | solution.py:69
  121.6 9.3 %slice-start = ((s8[8388608]{0:T(1024)(128)(4,1)}), s8[4194304]{0:T(1024)(128)(4,1)S(1)}, s32[]{:S(2)}) async-start(s8[8388608]{0:T(1024)(128)(4,1)} %bitcast.60), calls=%async_computation.6 | async-start | bytes 8388608
  121.6 9.3 %slice-start.1 = ((s8[8388608]{0:T(1024)(128)(4,1)}), s8[4194304]{0:T(1024)(128)(4,1)S(1)}, s32[]{:S(2)}) async-start(s8[8388608]{0:T(1024)(128)(4,1)} %bitcast.60), calls=%async_computation.7 | async-start | bytes 8388608
  182.5 19.2 %copy-start = (f32[64,64,128,1]{2,1,3,0:T(8,128)S(1)}, f32[64,64,128,1]{2,1,3,0:T(8,128)}, u32[]{:S(2)}) copy-start(f32[64,64,128,1]{2,1,3,0:T(8,128)} %get-tuple-element.5) | copy-start | bytes 6291460
  182.5 248.4 %reduce-scatter.5.cloned.1.call-start = ((), (), s32[]{:S(2)}) async-start(), calls=%async_computation.5 | async-start | bytes 4325376 | tf_op jit(solution)/shard_map/reduce_scatter | solution.py:72
  205.7 27.1 %collective-permute-start = (bf16[128,4096]{1,0:T(8,128)(2,1)S(1)}, bf16[128,4096]{1,0:T(8,128)(2,1)S(1)}, u32[]{:S(2)}, u32[]{:S(2)}) collective-permute-start(bf16[128,4096]{1,0:T(8,128)(2,1)S(1)} %fusion.5), channel_id=1, source_target_pairs={{64,0},{128,64},{192,128},{65,1},{129,65},{193,129},{66,2},{130,66... | collective-permute-start | bytes 3145736 | tf_op jit(solution)/shard_map/ppermute | solution.py:12
Sparse Core Ops, SparseCore 0:
  70.3 16.1 all-gather.1
  182.6 18.9 reduce-scatter.2
  206.1 224.7 reduce-scatter.4
